TPU v7x, 128 devices: a whole 4x4x4 slice. The times are simulated.
128 devices in a mesh: member: 8 (over x_hi, z), dp: 16 (over x_lo, y, core).
Axes of the slice: x: 4 (x_hi: 2, x_lo: 2; x = x_hi * 2 + x_lo), y: 4, z: 4, core: 2. Of those that a mesh axis runs over, the one named last changes fastest.
Arguments:
- latents: bfloat16 [8, 64, 16, 16, 640], P('member', 'dp'), may hold values from -6 to 6
- cotangent: bfloat16 [8, 64, 16, 16, 640], P('member', 'dp'), may hold values from -6 to 6
- weights: float32 [8, 640, 5760], P('member', 'dp'), may hold values from -6 to 6
- first_moment: float32 [8, 640, 5760], P('member', 'dp'), may hold values from -1.2 to 1.2
- second_moment: float32 [8, 640, 5760], P('member', 'dp'), may hold values from 0.02 to 0.5
- sources: int32 [8], replicated, may hold values from 0 to 7, as said below
Outputs:
- latent_grad: bfloat16 [8, 64, 16, 16, 640], P('member', 'dp')
- new_weights: float32 [8, 640, 5760], P('member', 'dp')
- new_first: float32 [8, 640, 5760], P('member', 'dp')
- new_second: float32 [8, 640, 5760], P('member', 'dp')
Inputs may be any that keep to these rules, and one draw needn't show every extreme that they name: sources[k] = k for every member that takes no copy; a member that takes a copy names a member that names itself; at most one quarter of the members (at least one) take copies, and at most one quarter (at least one) are named by others.
All inputs are finite; a program needn't handle non-finite values.
Results may differ from a plain program's by a relative error of at most 0.006.
Values may be sent and summed in bfloat16 or wider, within the bound.
No kernel may reach another device: no remote copies, remote signals or barrier semaphores. Data moves between devices by JAX's collectives and lax.ppermute only.
A program may use at most 128 MiB of HBM per device.

v0:
```python
import jax
import jax.numpy as jnp
from jax import lax
from jax.sharding import Mesh
from jax.sharding import PartitionSpec as P

CH_IN = 640
ADAM_STEP = 10


BETA_ONE = 0.9
BETA_TWO = 0.99
RATE = 0.05
EPSILON = 1e-08

MEMBER_AXES = ("x_hi", "z")
DP_AXES = ("x_lo", "y", "core")
TAP_GROUPS = ((0, 1, 2), (3, 4, 5), (6, 7, 8))


def silu_slope(values):
    sig = jax.nn.sigmoid(values)
    return sig * (1.0 + values * (1.0 - sig))


def shifted(padded, tap_index, side_cells, flip):
    tap_row = tap_index // 3
    tap_col = tap_index % 3
    if flip:
        tap_row = 2 - tap_row
        tap_col = 2 - tap_col
    window = padded[:, tap_row : tap_row + side_cells, tap_col : tap_col + side_cells, :]
    return window.reshape(-1, padded.shape[3])


def adam_update(weights_now, first_now, second_now, gradient):
    first_new = BETA_ONE * first_now + (1.0 - BETA_ONE) * gradient
    second_new = BETA_TWO * second_now + (1.0 - BETA_TWO) * gradient * gradient
    first_fix = 1.0 - BETA_ONE**ADAM_STEP
    second_fix = 1.0 - BETA_TWO**ADAM_STEP
    updated = weights_now - RATE * (first_new / first_fix) / (
        jnp.sqrt(second_new / second_fix) + EPSILON
    )
    return (updated, first_new, second_new)


def relocate(stacked, sources):
    members = lax.axis_size(MEMBER_AXES)
    layers = stacked.shape[0]
    shaped = stacked.reshape(layers, members, stacked.shape[1] // members, stacked.shape[2])
    held = lax.all_to_all(shaped, MEMBER_AXES, split_axis=1, concat_axis=1, tiled=True)
    picked = jnp.take(held, sources, axis=1)
    returned = lax.all_to_all(picked, MEMBER_AXES, split_axis=1, concat_axis=1, tiled=True)
    return returned.reshape(stacked.shape)


def gather_rows(rows):
    out = lax.all_gather(rows, "x_lo", axis=0, tiled=False)
    out = lax.all_gather(out, "y", axis=1, tiled=False)
    out = lax.all_gather(out, "core", axis=2, tiled=False)
    return out.reshape(-1, rows.shape[-1])


def scatter_rows(full):
    shaped = lax.psum_scatter(full, "core", scatter_dimension=0, tiled=True)
    shaped = lax.psum_scatter(shaped, "y", scatter_dimension=0, tiled=True)
    return lax.psum_scatter(shaped, "x_lo", scatter_dimension=0, tiled=True)


def local(latents, cotangent, weights, first_moment, second_moment, sources):
    scale = (9 * CH_IN) ** (-0.5)
    n_xlo = lax.axis_size("x_lo")
    n_y = lax.axis_size("y")
    n_core = lax.axis_size("core")
    images = latents[0]
    side_cells = images.shape[1]
    cell_count = images.shape[0] * side_cells * side_cells
    cols_out = cotangent.shape[4]

    moved_state = relocate(jnp.stack([weights[0], first_moment[0], second_moment[0]]), sources)

    activation = jax.nn.silu(images.astype(jnp.float32)).astype(jnp.bfloat16)
    kernel_rows = weights[0].astype(jnp.bfloat16)
    kernel_groups = []
    for group in TAP_GROUPS:
        lo = group[0] * cols_out
        hi = (group[-1] + 1) * cols_out
        kernel_groups.append(gather_rows(kernel_rows[:, lo:hi]))

    padded_act = jnp.pad(activation, ((0, 0), (1, 1), (1, 1), (0, 0)))
    summed = jnp.zeros((cell_count, cols_out), jnp.float32)
    for g, group in enumerate(TAP_GROUPS):
        for t, tap_index in enumerate(group):
            summed = summed + jnp.dot(
                shifted(padded_act, tap_index, side_cells, False),
                kernel_groups[g][:, t * cols_out : (t + 1) * cols_out],
                preferred_element_type=jnp.float32,
            )
    hidden = scale * summed
    deltas = (
        cotangent[0].reshape(cell_count, cols_out).astype(jnp.float32) * silu_slope(hidden)
    ).astype(jnp.bfloat16)
    deltas_img = deltas.reshape(cotangent[0].shape)

    lead = padded_act.shape[:3]
    padded_perm = (
        padded_act.reshape(lead + (n_xlo, n_y, n_core, -1))
        .transpose(0, 1, 2, 5, 4, 3, 6)
        .reshape(padded_act.shape)
    )
    grad_groups = []
    for g, group in enumerate(TAP_GROUPS):
        blocks = []
        for tap_index in group:
            blocks.append(
                lax.dot_general(
                    shifted(padded_perm, tap_index, side_cells, False),
                    deltas,
                    (((0,), (0,)), ((), ())),
                    preferred_element_type=jnp.float32,
                )
            )
        part = (scale * jnp.concatenate(blocks, axis=1)).astype(jnp.bfloat16)
        grad_groups.append(scatter_rows(part))

    padded_del = jnp.pad(deltas_img, ((0, 0), (1, 1), (1, 1), (0, 0)))
    back = jnp.zeros((cell_count, images.shape[3]), jnp.float32)
    for g, group in enumerate(TAP_GROUPS):
        for t, tap_index in enumerate(group):
            back = back + lax.dot_general(
                shifted(padded_del, tap_index, side_cells, True),
                kernel_groups[g][:, t * cols_out : (t + 1) * cols_out],
                (((1,), (1,)), ((), ())),
                preferred_element_type=jnp.float32,
            )
    back = scale * back
    slope_in = silu_slope(images.reshape(cell_count, images.shape[3]).astype(jnp.float32))
    latent_grad = (back * slope_in).astype(jnp.bfloat16).reshape(latents.shape)

    gradient_bf = jnp.concatenate(grad_groups, axis=1)
    moved_grad = relocate(gradient_bf[None], sources)[0].astype(jnp.float32)
    updated, first_new, second_new = adam_update(
        moved_state[0], moved_state[1], moved_state[2], moved_grad
    )
    return (latent_grad, updated[None], first_new[None], second_new[None])


def solution(mesh):
    sub_mesh = Mesh(
        mesh.devices.reshape(2, mesh.shape["member"] // 2, 2, mesh.shape["dp"] // 4, 2),
        MEMBER_AXES + DP_AXES,
    )
    big = P(MEMBER_AXES, DP_AXES, None, None, None)
    state = P(MEMBER_AXES, DP_AXES, None)
    in_specs = (big, big, state, state, state, P())
    out_specs = (big, state, state, state)
    return jax.shard_map(local, mesh=sub_mesh, in_specs=in_specs, out_specs=out_specs, check_vma=False)
```

profile of v0, /device:TPU:0, one launch (start us, length us, event | category | flops | bytes accessed | tf_op | source)
XLA Modules:
  0.0 465.4 jit_solution(15336084750233568795)
XLA Ops:
  8.5 6.3 %all-gather.6 = bf16[80,1920]{1,0:T(8,128)(2,1)} all-gather(bf16[40,1920]{1,0:T(8,128)(2,1)S(1)} %get-tuple-element.51), channel_id=8, replica_groups=mesh['x_hi'=2,'z'=4,'x_lo'=2,'y'=4,'core'=2] {'x_lo'}, dimensions={0}, use_global_device_ids=true | all-gather | bytes 460800 | tf_op jit(solution)/shard_map/all_gather | solution.py:58
  14.9 6.0 %all-gather.3 = bf16[80,1920]{1,0:T(8,128)(2,1)} all-gather(bf16[40,1920]{1,0:T(8,128)(2,1)S(1)} %get-tuple-element.52), channel_id=5, replica_groups=mesh['x_hi'=2,'z'=4,'x_lo'=2,'y'=4,'core'=2] {'x_lo'}, dimensions={0}, use_global_device_ids=true | all-gather | bytes 460800 | tf_op jit(solution)/shard_map/all_gather | solution.py:58
  21.0 6.1 %all-gather = bf16[80,1920]{1,0:T(8,128)(2,1)} all-gather(bf16[40,1920]{1,0:T(8,128)(2,1)S(1)} %get-tuple-element.50), channel_id=2, replica_groups=mesh['x_hi'=2,'z'=4,'x_lo'=2,'y'=4,'core'=2] {'x_lo'}, dimensions={0}, use_global_device_ids=true | all-gather | bytes 460800 | tf_op jit(solution)/shard_map/all_gather | solution.py:58
  27.2 15.0 %all-gather.24.cloned.1.call-done = bf16[2,160,1920]{2,1,0:T(8,128)(2,1)} async-done(((bf16[2,40,1920]{2,1,0:T(8,128)(2,1)}), bf16[2,160,1920]{2,1,0:T(8,128)(2,1)}) %all-gather.24.cloned.1.call-update) | async-done | bytes 1228816 | tf_op jit(solution)/shard_map/all_gather | solution.py:59
  42.2 26.8 %all-gather.20.cloned.1.call-done = bf16[2,160,1920]{2,1,0:T(8,128)(2,1)} async-done(((bf16[2,40,1920]{2,1,0:T(8,128)(2,1)}), bf16[2,160,1920]{2,1,0:T(8,128)(2,1)}) %all-gather.20.cloned.1.call-update) | async-done | bytes 1228816 | tf_op jit(solution)/shard_map/all_gather | solution.py:59
  72.6 9.1 %reshape.252 = bf16[4,18,18,2,4,2,40]{6,5,4,3,0,2,1:T(2,128)(2,1)} reshape(bf16[4,18,18,640]{3,0,2,1:T(4,128)(2,1)S(1)} %pad.7.clone) | data formatting | bytes 3317760 | tf_op jit(solution)/shard_map/reshape | solution.py:107
  81.6 10.7 %copy.36 = bf16[4,18,18,2,4,2,40]{6,5,4,3,0,2,1:T(2,128)(2,1)} copy(bf16[4,18,18,2,4,2,40]{6,3,4,5,0,2,1:T(2,128)(2,1)} %bitcast.155) | data formatting | bytes 3317760 | tf_op jit(solution)/shard_map/transpose | solution.py:108
  92.3 17.3 %reshape.253 = bf16[4,18,18,640]{3,0,2,1:T(4,128)(2,1)S(1)} reshape(bf16[4,18,18,2,4,2,40]{6,5,4,3,0,2,1:T(2,128)(2,1)} %copy.36) | data formatting | bytes 3317760 | tf_op jit(solution)/shard_map/reshape | solution.py:109
  109.9 5.6 %fusion.55 = (bf16[4,16,16,640]{3,0,2,1:T(4,128)(2,1)S(1)}, bf16[4,16,16,640]{3,0,2,1:T(4,128)(2,1)}, bf16[4,16,16,640]{3,0,2,1:T(4,128)(2,1)}, bf16[4,16,16,640...) fusion(bf16[4,18,18,640]{3,0,2,1:T(4,128)(2,1)S(1)} %reshape.253), kind=kLoop, calls=%fused_computation.96 | loop fusion | bytes 23592960 | tf_op jit(solution)/shard_map/slice | solution.py:32
  119.7 4.5 pad_slice_fusion.8
  124.2 1.9 fusion.13
  126.1 4.8 %fusion.24 = f32[1024,640]{1,0:T(8,128)} fusion(bf16[1024,640]{1,0:T(8,128)(2,1)} %bitcast.182, bf16[640,1920]{1,0:T(8,128)(2,1)} %bitcast.191), kind=kOutput, calls=%fused_computation.58 | convolution fusion | flops 838860800 | bytes 4751360 | tf_op jit(solution)/shard_map/dot_general | solution.py:94
  130.9 3.9 fusion.28
  134.8 4.5 fusion.32
  139.3 4.0 fusion.40
  143.4 2.0 all-gather.18.cloned.1.call-done
  145.4 3.0 fusion.44
  148.4 1.3 fusion.48
  149.8 1.3 fusion.52
  151.1 2.7 fusion.36
  155.1 4.1 fusion.3
  159.2 3.0 fusion.57
  164.8 2.0 fusion
  166.8 4.4 copy.55
  171.3 1.6 copy.40
  177.2 1.3 fusion.62
  178.4 1.9 fusion.1
  180.4 4.5 copy.61
  185.2 1.7 copy.43
  192.4 2.0 fusion.2
  194.4 4.4 copy.67
  199.4 3.1 reduce-scatter.26.cloned.1.call-done
  202.6 1.9 pad_maximum_fusion
  204.5 2.8 copy.54
  207.3 7.1 %all-to-all-start = ((f32[3,8,5,5760]{3,0,2,1:T(4,128)}), f32[3,8,5,5760]{3,0,2,1:T(4,128)}, u32[]{:S(2)}, u32[]{:S(2)}) async-start(f32[3,8,5,5760]{3,0,2,1:T(4,128)} %bitcast.156), calls=%async_computation | async-start | bytes 7372800 | tf_op jit(solution)/shard_map/all_to_all | solution.py:51
  215.7 42.5 %all-to-all-done = f32[3,8,5,5760]{3,0,2,1:T(4,128)} async-done(((f32[3,8,5,5760]{3,0,2,1:T(4,128)}), f32[3,8,5,5760]{3,0,2,1:T(4,128)}, u32[]{:S(2)}, u32[]{:S(2)}) %all-to-all-start) | async-done | bytes 2764832 | tf_op jit(solution)/shard_map/all_to_all | solution.py:51
  258.2 6.4 %gather_fusion = f32[8,3,5,5760]{3,1,2,0:T(4,128)} fusion(f32[3,8,5,5760]{3,0,2,1:T(4,128)} %all-to-all-done, s32[1024]{0:T(1024)S(1)} %pad_clamp_fusion), kind=kCustom, calls=%fused_computation | custom fusion | bytes 5529632 | tf_op jit(solution)/shard_map/jit(_take)/gather | solution.py:52
  265.0 4.9 %select_bitcast_fusion = f32[3,8,5,5760]{3,0,2,1:T(4,128)} fusion(f32[8,3,5,5760]{3,1,2,0:T(4,128)} %gather_fusion, pred[8]{0:T(512)(128)(4,1)S(1)} %compare_and_fusion), kind=kLoop, calls=%fused_computation.8 | loop fusion | flops 691200 | bytes 5529608 | tf_op jit(solution)/shard_map/jit(_take)/select_n | solution.py:52
  269.9 2.9 fusion.34
  272.7 4.4 pad_slice_fusion
  277.1 4.0 fusion.26
  281.1 2.9 fusion.30
  284.0 2.0 copy.58
  286.0 2.1 copy.64
  288.0 12.5 %reduce-scatter.32.cloned.1.call-done = bf16[80,1920]{1,0:T(8,128)(2,1)} async-done(((bf16[320,1920]{1,0:T(8,128)(2,1)}), bf16[80,1920]{1,0:T(8,128)(2,1)}) %reduce-scatter.32.cloned.1.call-update) | async-done | bytes 307216
  300.6 2.0 copy.70
  302.6 4.1 fusion.38
  306.7 2.9 fusion.42
  309.6 2.9 fusion.46
  312.5 47.1 %all-reduce.8.cloned.1.call-done = (bf16[80,1920]{0,1:T(8,128)(2,1)}, bf16[80,1920]{0,1:T(8,128)(2,1)}, bf16[80,1920]{0,1:T(8,128)(2,1)}) async-done(((bf16[80,1920]{0,1:T(8,128)(2,1)}, bf16[80,1920]{0,1:T(8,128)(2,1)}, bf16[80,1920]{0,1:T(8,128)(2,1)}), (bf16[80,1920]{0,1:T(8,128)(2,1)}, bf16[80,1920]{0,1:T(8,128)(2,1)}, bf16[80,1920]{0,1:T(8,128)(2,1)})) %all-reduce.8.cloned.1.call-update) | async-done | bytes 921616
  359.5 1.6 constant_dynamic-slice_fusion
  363.1 6.9 %all-to-all-start.2 = ((bf16[1,8,5,5760]{3,2,0,1:T(8,128)(2,1)}), bf16[1,8,5,5760]{3,2,0,1:T(8,128)(2,1)}, u32[]{:S(2)}, u32[]{:S(2)}) async-start(bf16[1,8,5,5760]{3,2,0,1:T(8,128)(2,1)} %bitcast.45), calls=%async_computation.2 | async-start | bytes 1474560 | tf_op jit(solution)/shard_map/all_to_all | solution.py:51
  369.9 4.5 fusion.50
  374.4 4.0 fusion.22
  378.4 4.3 all-to-all-done.2
  382.7 4.5 all-to-all-start.1
  387.2 9.4 %fusion.17 = bf16[1024,640]{1,0:T(8,128)(2,1)} fusion(bf16[1,4,16,16,640]{4,3,2,1,0:T(8,128)(2,1)S(1)} %copy-done, f32[1024,640]{1,0:T(8,128)} %fusion.22, f32[1024,640]{1,0:T(8,128)} %fusion.26, f32[1024,640]{1,0:T(8,128)} %fusion.30, f32[1024,640]{1,0:T(8,128)} %fusion.34, f32[1024,640]{1,0:T(8,128)} %fusion.38, f32[1024,640]{1,0:T(8,128)} %fusion.42, ...), kind=kOutput, calls=%fused_computation.37 | convolution fusion | flops 851312640 | bytes 25722880 | tf_op jit(solution)/shard_map/dot_general | solution.py:130
  396.6 1.8 gather_fusion.1
  399.4 30.7 %all-to-all-done.1 = f32[3,8,5,5760]{3,0,2,1:T(4,128)} async-done(((f32[3,8,5,5760]{3,0,2,1:T(4,128)}), f32[3,8,5,5760]{3,0,2,1:T(4,128)}, u32[]{:S(2)}, u32[]{:S(2)}) %all-to-all-start.1) | async-done | bytes 2764832 | tf_op jit(solution)/shard_map/all_to_all | solution.py:53
  430.1 4.8 %all-to-all-start.3 = ((bf16[1,8,5,5760]{3,2,0,1:T(8,128)(2,1)}), bf16[1,8,5,5760]{3,2,0,1:T(8,128)(2,1)S(1)}, u32[]{:S(2)}, u32[]{:S(2)}) async-start(bf16[1,8,5,5760]{3,2,0,1:T(8,128)(2,1)} %fusion.19), calls=%async_computation.3 | async-start | bytes 1474560 | tf_op jit(solution)/shard_map/all_to_all | solution.py:53
  434.9 7.7 %slice_multiply_fusion = (f32[1,8,5,5760]{3,0,2,1:T(1,128)S(1)}, f32[1,8,5,5760]{3,0,2,1:T(1,128)S(1)}, f32[1,8,5,5760]{3,0,2,1:T(1,128)S(1)}) fusion(f32[3,8,5,5760]{3,0,2,1:T(4,128)} %all-to-all-done.1), kind=kLoop, calls=%fused_computation.48 | loop fusion | flops 460800 | bytes 5529600 | tf_op jit(solution)/shard_map/mul | solution.py:38
  442.6 5.4 %all-to-all-done.3 = bf16[1,8,5,5760]{3,2,0,1:T(8,128)(2,1)S(1)} async-done(((bf16[1,8,5,5760]{3,2,0,1:T(8,128)(2,1)}), bf16[1,8,5,5760]{3,2,0,1:T(8,128)(2,1)S(1)}, u32[]{:S(2)}, u32[]{:S(2)}) %all-to-all-start.3) | async-done | bytes 460832 | tf_op jit(solution)/shard_map/all_to_all | solution.py:53
  448.0 2.0 reshape.266
  449.9 5.6 %bitcast_subtract_fusion = (f32[1,40,5760]{2,0,1:T(1,128)S(1)}, f32[1,40,5760]{2,0,1:T(1,128)S(1)}, f32[1,40,5760]{2,0,1:T(1,128)S(1)}) fusion(f32[1,8,5,5760]{3,0,2,1:T(1,128)S(1)} %get-tuple-element.24, f32[1,40,5760]{2,0,1:T(1,128)} %reshape.266, f32[1,8,5,5760]{3,0,2,1:T(1,128)S(1)} %get-tuple-element.23, f32[1,8,5,5760]{3,0,2,1:T(1,128)S(1)} %get-tuple-element.22), kind=kLoop, calls=%fused_computation.51 | loop fusion | flops 2304000 | bytes 6451200 | tf_op jit(solution)/shard_map/sub | solution.py:41
  (132 shorter events, 30.9 us)
Async XLA Ops:
  7.2 35.0 %all-gather.24.cloned.1.call-start = ((), (), s32[]{:S(2)}) async-start(), calls=%async_computation.14 | async-start | bytes 1536000 | tf_op jit(solution)/shard_map/all_gather | solution.py:59
  14.9 54.2 %all-gather.20.cloned.1.call-start = ((), (), s32[]{:S(2)}) async-start(), calls=%async_computation.12 | async-start | bytes 1536000 | tf_op jit(solution)/shard_map/all_gather | solution.py:59
  20.9 48.2 %copy-start = (bf16[1,4,16,16,640]{4,3,2,1,0:T(8,128)(2,1)S(1)}, bf16[1,4,16,16,640]{4,3,2,1,0:T(8,128)(2,1)}, u32[]{:S(2)}) copy-start(bf16[1,4,16,16,640]{4,3,2,1,0:T(8,128)(2,1)} %param.6) | copy-start | bytes 3932164
  20.9 88.7 %all-gather.16.cloned.1.call-start = ((), (), s32[]{:S(2)}) async-start(), calls=%async_computation.10 | async-start | bytes 1536000 | tf_op jit(solution)/shard_map/all_gather | solution.py:59
  27.1 99.0 %all-gather.26.cloned.1.call-start = ((), (), s32[]{:S(2)}) async-start(), calls=%async_computation.15 | async-start | bytes 3686400 | tf_op jit(solution)/shard_map/all_gather | solution.py:60
  42.2 92.7 %all-gather.22.cloned.1.call-start = ((), (), s32[]{:S(2)}) async-start(), calls=%async_computation.13 | async-start | bytes 3686400 | tf_op jit(solution)/shard_map/all_gather | solution.py:60
  69.1 76.3 %all-gather.18.cloned.1.call-start = ((), (), s32[]{:S(2)}) async-start(), calls=%async_computation.11 | async-start | bytes 3686400 | tf_op jit(solution)/shard_map/all_gather | solution.py:60
  69.9 1.1 copy-start.1
  109.6 89.3 %reduce-scatter.22.cloned.1.call-start = ((), (), s32[]{:S(2)}) async-start(), calls=%async_computation.16 | async-start | bytes 3686400
  117.9 1.8 copy-start.2
  126.1 4.8 %copy-start.26 = (bf16[4,16,16,640]{3,2,1,0:T(8,128)(2,1)S(1)}, bf16[4,16,16,640]{3,2,1,0:T(8,128)(2,1)}, u32[]{:S(2)}) copy-start(bf16[4,16,16,640]{3,2,1,0:T(8,128)(2,1)} %get-tuple-element.48) | copy-start | bytes 3932164
  134.8 4.5 copy-start.25
  145.4 3.0 copy-start.24
  145.4 3.0 copy-start.28
  148.4 1.3 copy-start.23
  149.7 1.3 copy-start.18
  149.8 4.1 copy-start.14
  149.8 4.1 copy-start.15
  151.1 2.7 copy-start.11
  151.1 3.2 copy-start.12
  151.1 3.9 copy-start.13
  159.1 4.3 copy-start.7
  159.1 3.1 copy-start.16
  162.2 1.3 copy-start.17
  171.2 1.7 copy-start.6
  171.2 31.4 %reduce-scatter.26.cloned.1.call-start = ((), (), s32[]{:S(2)}) async-start(), calls=%async_computation.18 | async-start | bytes 3686400
  172.8 1.3 copy-start.5
  173.1 1.5 copy-start.8
  184.9 1.9 copy-start.4
  184.9 79.7 %reduce-scatter.30.cloned.1.call-start = ((), (), s32[]{:S(2)}) async-start(), calls=%async_computation.20 | async-start | bytes 3686400
  186.8 1.3 copy-start.3
  187.0 1.6 copy-start.9
  198.8 85.2 %reduce-scatter.24.cloned.1.call-start = ((), (), s32[]{:S(2)}) async-start(), calls=%async_computation.17 | async-start | bytes 1536000
  199.4 86.6 %reduce-scatter.28.cloned.1.call-start = ((), (), s32[]{:S(2)}) async-start(), calls=%async_computation.19 | async-start | bytes 1536000
  207.3 7.1 %copy-start.32 = (u32[128]{0:T(128)S(1)}, u32[128]{0:T(128)}, u32[]{:S(2)}) copy-start(u32[128]{0:T(128)} %constant.68) | copy-start | bytes 1540
  207.3 8.4 %copy-start.31 = (s32[8]{0:T(128)S(1)}, s32[8]{0:T(128)}, u32[]{:S(2)}) copy-start(s32[8]{0:T(128)} %param.11) | copy-start | bytes 100
  207.3 50.9 %all-to-all-start = ((f32[3,8,5,5760]{3,0,2,1:T(4,128)}), f32[3,8,5,5760]{3,0,2,1:T(4,128)}, u32[]{:S(2)}, u32[]{:S(2)}) async-start(f32[3,8,5,5760]{3,0,2,1:T(4,128)} %bitcast.156), calls=%async_computation | async-start | bytes 7372800 | tf_op jit(solution)/shard_map/all_to_all | solution.py:51
  214.4 86.2 %reduce-scatter.32.cloned.1.call-start = ((), (), s32[]{:S(2)}) async-start(), calls=%async_computation.21 | async-start | bytes 1536000
  264.7 94.8 %all-reduce.8.cloned.1.call-start = ((), (), s32[]{:S(2)}) async-start(), calls=%async_computation.22 | async-start | bytes 2949120
  265.0 4.9 %copy-start.30 = (bf16[2,4,80,1920]{3,2,1,0:T(8,128)(2,1)S(1)}, bf16[2,4,80,1920]{3,2,1,0:T(8,128)(2,1)}, u32[]{:S(2)}) copy-start(bf16[2,4,80,1920]{3,2,1,0:T(8,128)(2,1)} %all-gather.22.cloned.1.call-done) | copy-start | bytes 7372804
  286.0 16.6 %copy-start.22 = (bf16[4,16,16,640]{3,2,1,0:T(8,128)(2,1)S(1)}, bf16[4,16,16,640]{3,2,1,0:T(8,128)(2,1)}, u32[]{:S(2)}) copy-start(bf16[4,16,16,640]{3,2,1,0:T(8,128)(2,1)} %get-tuple-element.37) | copy-start | bytes 3932164
  302.5 4.1 copy-start.21
  302.6 4.1 copy-start.29
  306.7 2.9 copy-start.20
  359.5 2.0 copy-start.27
  363.1 19.7 %all-to-all-start.2 = ((bf16[1,8,5,5760]{3,2,0,1:T(8,128)(2,1)}), bf16[1,8,5,5760]{3,2,0,1:T(8,128)(2,1)}, u32[]{:S(2)}, u32[]{:S(2)}) async-start(bf16[1,8,5,5760]{3,2,0,1:T(8,128)(2,1)} %bitcast.45), calls=%async_computation.2 | async-start | bytes 1474560 | tf_op jit(solution)/shard_map/all_to_all | solution.py:51
  369.9 4.5 copy-start.19
  378.4 8.9 %copy-start.10 = (bf16[4,16,16,640]{3,2,1,0:T(8,128)(2,1)S(1)}, bf16[4,16,16,640]{3,2,1,0:T(8,128)(2,1)}, u32[]{:S(2)}) copy-start(bf16[4,16,16,640]{3,2,1,0:T(8,128)(2,1)} %get-tuple-element.34) | copy-start | bytes 3932164
  382.7 47.4 %all-to-all-start.1 = ((f32[3,8,5,5760]{3,0,2,1:T(4,128)}), f32[3,8,5,5760]{3,0,2,1:T(4,128)}, u32[]{:S(2)}, u32[]{:S(2)}) async-start(f32[3,8,5,5760]{3,0,2,1:T(4,128)} %select_bitcast_fusion), calls=%async_computation.1 | async-start | bytes 7372800 | tf_op jit(solution)/shard_map/all_to_all | solution.py:53
  430.1 17.9 %all-to-all-start.3 = ((bf16[1,8,5,5760]{3,2,0,1:T(8,128)(2,1)}), bf16[1,8,5,5760]{3,2,0,1:T(8,128)(2,1)S(1)}, u32[]{:S(2)}, u32[]{:S(2)}) async-start(bf16[1,8,5,5760]{3,2,0,1:T(8,128)(2,1)} %fusion.19), calls=%async_computation.3 | async-start | bytes 1474560 | tf_op jit(solution)/shard_map/all_to_all | solution.py:53
Sparse Core Ops, SparseCore 0:
  15.0 27.1 all-gather.23
  43.8 25.1 all-gather.19
  70.8 25.1 all-gather.15
  97.5 14.4 all-gather.25
  113.5 15.1 all-gather.21
  130.2 15.1 all-gather.17
  171.3 14.3 reduce-scatter.21
  188.1 14.3 reduce-scatter.25
  205.0 14.3 reduce-scatter.29
  221.7 25.7 reduce-scatter.23
  249.9 24.1 reduce-scatter.27
  276.4 24.1 reduce-scatter.31
  303.8 55.7 all-reduce.7
where the time goes:
time: 474 us; the launch traced here: 465 us
  waiting for transfers between devices  190 us (40%)
  local copies, waits for them, and re-layouts  106 us (22%)
  matrix products  80.1 us (17%)
  other arithmetic  30.9 us (7%)
  starting transfers between devices  24.3 us (5%)
  blocking collectives  18.4 us (4%)
  between operations  15.6 us (3%)
    unnamed x20, waiting for transfers between devices  63.4 us
    all_to_all x2, waiting for transfers between devices, relocate(): lax.all_to_all(shaped, MEMBER_AXES, split_axis=1, concat_axis=1, tiled=True)  46.8 us
    all_gather x3, waiting for transfers between devices, gather_rows(): out = lax.all_gather(out, 'y', axis=1, tiled=False)  41.9 us
    dot_general x9, matrix products, local(): lax.dot_general(shifted(padded_del, tap_index, side_cells, True), kernel_...  37.4 us
    all_to_all x2, waiting for transfers between devices, relocate(): lax.all_to_all(picked, MEMBER_AXES, split_axis=1, concat_axis=1, tiled=True)  36.1 us
    unnamed x79, local copies, waits for them, and re-layouts  31.4 us
    dot_general x9, matrix products, local(): jnp.dot(shifted(padded_act, tap_index, side_cells, False), kernel_groups[...  29.6 us
    slice x12, local copies, waits for them, and re-layouts, shifted(): padded[:, tap_row:tap_row + side_cells, tap_col:tap_col + side_cells, :]  22.1 us
  transfers between devices with their start and end apart: 17, of which 10 were waited for; matrix products, arithmetic and copies ran while one was open for 36% of the time, Pallas kernels for 0%

commit v1 on v0

--- a/solution.py
+++ b/solution.py
@@ -44,40 +44,41 @@
     return (updated, first_new, second_new)
 
 
-def relocate(stacked, sources):
+def to_holders(stacked):
     members = lax.axis_size(MEMBER_AXES)
     layers = stacked.shape[0]
     shaped = stacked.reshape(layers, members, stacked.shape[1] // members, stacked.shape[2])
-    held = lax.all_to_all(shaped, MEMBER_AXES, split_axis=1, concat_axis=1, tiled=True)
+    return lax.all_to_all(shaped, MEMBER_AXES, split_axis=1, concat_axis=1, tiled=True)
+
+
+def from_holders(held, sources):
     picked = jnp.take(held, sources, axis=1)
     returned = lax.all_to_all(picked, MEMBER_AXES, split_axis=1, concat_axis=1, tiled=True)
-    return returned.reshape(stacked.shape)
+    return returned.reshape(returned.shape[0], -1, returned.shape[3])
+
+
+def relocate(stacked, sources):
+    return from_holders(to_holders(stacked), sources)
 
 
 def gather_rows(rows):
-    out = lax.all_gather(rows, "x_lo", axis=0, tiled=False)
-    out = lax.all_gather(out, "y", axis=1, tiled=False)
-    out = lax.all_gather(out, "core", axis=2, tiled=False)
-    return out.reshape(-1, rows.shape[-1])
+    return lax.all_gather(rows, DP_AXES, axis=0, tiled=True)
 
 
 def scatter_rows(full):
-    shaped = lax.psum_scatter(full, "core", scatter_dimension=0, tiled=True)
-    shaped = lax.psum_scatter(shaped, "y", scatter_dimension=0, tiled=True)
-    return lax.psum_scatter(shaped, "x_lo", scatter_dimension=0, tiled=True)
+    n_dp = lax.axis_size(DP_AXES)
+    blocks = full.reshape(n_dp, full.shape[0] // n_dp, full.shape[1])
+    return lax.psum_scatter(blocks, DP_AXES, scatter_dimension=0, tiled=True)[0]
 
 
 def local(latents, cotangent, weights, first_moment, second_moment, sources):
     scale = (9 * CH_IN) ** (-0.5)
-    n_xlo = lax.axis_size("x_lo")
-    n_y = lax.axis_size("y")
-    n_core = lax.axis_size("core")
     images = latents[0]
     side_cells = images.shape[1]
     cell_count = images.shape[0] * side_cells * side_cells
     cols_out = cotangent.shape[4]
 
-    moved_state = relocate(jnp.stack([weights[0], first_moment[0], second_moment[0]]), sources)
+    held_state = to_holders(jnp.stack([weights[0], first_moment[0], second_moment[0]]))
 
     activation = jax.nn.silu(images.astype(jnp.float32)).astype(jnp.bfloat16)
     kernel_rows = weights[0].astype(jnp.bfloat16)
@@ -88,6 +89,8 @@
         kernel_groups.append(gather_rows(kernel_rows[:, lo:hi]))
 
     padded_act = jnp.pad(activation, ((0, 0), (1, 1), (1, 1), (0, 0)))
+    held_state, padded_act = lax.optimization_barrier((held_state, padded_act))
+    moved_state = from_holders(held_state, sources)
     summed = jnp.zeros((cell_count, cols_out), jnp.float32)
     for g, group in enumerate(TAP_GROUPS):
         for t, tap_index in enumerate(group):
@@ -100,21 +103,16 @@
     deltas = (
         cotangent[0].reshape(cell_count, cols_out).astype(jnp.float32) * silu_slope(hidden)
     ).astype(jnp.bfloat16)
+    moved_state, deltas = lax.optimization_barrier((moved_state, deltas))
     deltas_img = deltas.reshape(cotangent[0].shape)
 
-    lead = padded_act.shape[:3]
-    padded_perm = (
-        padded_act.reshape(lead + (n_xlo, n_y, n_core, -1))
-        .transpose(0, 1, 2, 5, 4, 3, 6)
-        .reshape(padded_act.shape)
-    )
     grad_groups = []
     for g, group in enumerate(TAP_GROUPS):
         blocks = []
         for tap_index in group:
             blocks.append(
                 lax.dot_general(
-                    shifted(padded_perm, tap_index, side_cells, False),
+                    shifted(padded_act, tap_index, side_cells, False),
                     deltas,
                     (((0,), (0,)), ((), ())),
                     preferred_element_type=jnp.float32,

time: 474 us -> 419 us (0.88)
  local copies, waits for them, and re-layouts: 106 us -> 52.4 us
  waiting for transfers between devices: 190 us -> 218 us
  blocking collectives: 18.4 us -> 0 us
  other arithmetic: 30.9 us -> 19.9 us
    unnamed x20 -> x9, waiting for transfers between devices: 63.4 us -> 143 us
    all_gather x6 -> x3, waiting for transfers between devices: 43.9 us -> 0.01 us  [gather_rows(): return lax.all_gather(rows, DP_AXES, axis=0, tiled=True)]
    unnamed x79 -> x68, local copies, waits for them, and re-layouts: 31.4 us -> 4.01 us
    all_gather x3 -> x0, blocking collectives: 18.4 us -> none  [gather_rows(): out = lax.all_gather(rows, 'x_lo', axis=0, tiled=False)]
    slice x12 -> x2, local copies, waits for them, and re-layouts: 22.1 us -> 9.23 us  [shifted(): padded[:, tap_row:tap_row + side_cells, tap_col:tap_col + side_cells, :]]
    transpose x1 -> x0, local copies, waits for them, and re-layouts: 10.7 us -> none  [local(): padded_perm = padded_act.reshape(lead + (n_xlo, n_y, n_core, -1)).transpo...]
    mul x1 -> x0, other arithmetic: 7.72 us -> none  [adam_update(): second_new = BETA_TWO * second_now + (1.0 - BETA_TWO) * gradient * gradient]
    all_to_all x4, waiting for transfers between devices: 82.9 us -> 75.3 us  [the longest x2 65.2 us: to_holders(): lax.all_to_all(shaped, MEMBER_AXES, split_axis=1, concat_axis=1, tiled=True)]
  transfers between devices with their start and end apart: 17 -> 10, of which waited for: 10 -> 6; matrix products, arithmetic and copies ran while one was open for 36% -> 32% of each run, Pallas kernels for 0% -> 0%
where the time goes in v1:
time: 419 us; the launch traced here: 413 us
  waiting for transfers between devices  218 us (52%)
  matrix products  82.9 us (20%)
  local copies, waits for them, and re-layouts  52.4 us (13%)
  starting transfers between devices  24.5 us (6%)
  other arithmetic  19.9 us (5%)
  between operations  14.7 us (4%)
    unnamed x9, waiting for transfers between devices  143 us
    all_to_all x2, waiting for transfers between devices, to_holders(): lax.all_to_all(shaped, MEMBER_AXES, split_axis=1, concat_axis=1, tiled=True)  65.2 us
    dot_general x9, matrix products, local(): lax.dot_general(shifted(padded_del, tap_index, side_cells, True), kernel_...  39.8 us
    dot_general x9, matrix products, local(): jnp.dot(shifted(padded_act, tap_index, side_cells, False), kernel_groups[...  28.5 us
    reshape x9, local copies, waits for them, and re-layouts, shifted(): return window.reshape(-1, padded.shape[3])  20.5 us
    dot_general x9, matrix products, local(): lax.dot_general(shifted(padded_act, tap_index, side_cells, False), deltas...  14.6 us
    all_to_all x2, starting transfers between devices, to_holders(): lax.all_to_all(shaped, MEMBER_AXES, split_axis=1, concat_axis=1, tiled=True)  14.6 us
    all_to_all x2, waiting for transfers between devices, from_holders(): lax.all_to_all(picked, MEMBER_AXES, split_axis=1, concat_axis=1, tiled=True)  10.1 us
  transfers between devices with their start and end apart: 10, of which 6 were waited for; matrix products, arithmetic and copies ran while one was open for 32% of the time, Pallas kernels for 0%

profile of v1, /device:TPU:0, one launch (start us, length us, event | category | flops | bytes accessed | tf_op | source)
XLA Modules:
  0.0 412.8 jit_solution(14041161600902101986)
XLA Ops:
  7.2 1.4 convert_bitcast_fusion.1
  10.2 1.4 pad_maximum_fusion
  11.5 2.8 copy.49
  14.3 8.0 %all-to-all-start = ((f32[3,8,5,5760]{3,0,2,1:T(4,128)}), f32[3,8,5,5760]{3,0,2,1:T(4,128)}, u32[]{:S(2)}, u32[]{:S(2)}) async-start(f32[3,8,5,5760]{3,0,2,1:T(4,128)} %bitcast.147), calls=%async_computation | async-start | bytes 7372800 | tf_op jit(solution)/shard_map/all_to_all | solution.py:51
  24.7 63.1 %all-to-all-done = f32[3,8,5,5760]{3,0,2,1:T(4,128)} async-done(((f32[3,8,5,5760]{3,0,2,1:T(4,128)}), f32[3,8,5,5760]{3,0,2,1:T(4,128)}, u32[]{:S(2)}, u32[]{:S(2)}) %all-to-all-start) | async-done | bytes 2764832 | tf_op jit(solution)/shard_map/all_to_all | solution.py:51
  87.8 6.4 %gather_fusion = f32[8,3,5,5760]{3,1,2,0:T(4,128)} fusion(f32[3,8,5,5760]{3,0,2,1:T(4,128)} %all-to-all-done, s32[1024]{0:T(1024)S(1)} %pad_clamp_fusion), kind=kCustom, calls=%fused_computation | custom fusion | bytes 5529632 | tf_op jit(solution)/shard_map/jit(_take)/gather | solution.py:55
  94.1 4.7 %select_bitcast_fusion = f32[3,8,5,5760]{3,0,2,1:T(4,128)} fusion(f32[8,3,5,5760]{3,1,2,0:T(4,128)} %gather_fusion, pred[8]{0:T(512)(128)(4,1)S(1)} %compare_and_fusion), kind=kLoop, calls=%fused_computation.8 | loop fusion | flops 691200 | bytes 5529608 | tf_op jit(solution)/shard_map/jit(_take)/select_n | solution.py:55
  98.9 4.5 %all-to-all-start.1 = ((f32[3,8,5,5760]{3,0,2,1:T(4,128)}), f32[3,8,5,5760]{3,0,2,1:T(4,128)}, u32[]{:S(2)}, u32[]{:S(2)}) async-start(f32[3,8,5,5760]{3,0,2,1:T(4,128)} %select_bitcast_fusion), calls=%async_computation.1 | async-start | bytes 7372800 | tf_op jit(solution)/shard_map/all_to_all | solution.py:56
  103.6 4.8 %fusion.72 = (bf16[4,16,16,640]{3,2,1,0:T(8,128)(2,1)S(1)}, bf16[4,16,16,640]{3,2,1,0:T(8,128)(2,1)}, bf16[4,16,16,640]{3,2,1,0:T(8,128)(2,1)}, bf16[4,16,16,640...) fusion(bf16[4,18,18,640]{3,2,1,0:T(8,128)(2,1)S(1)} %pad.7), kind=kLoop, calls=%fused_computation.99 | loop fusion | bytes 23592960 | tf_op jit(solution)/shard_map/slice | solution.py:32
  108.4 1.6 copy.43
  110.0 2.5 copy.42
  112.5 1.6 copy.41
  114.0 4.6 %fusion.41 = f32[1024,640]{1,0:T(8,128)} fusion(bf16[1024,640]{1,0:T(8,128)(2,1)} %bitcast.165, bf16[640,1920]{1,0:T(8,128)(2,1)} %all-gather.8.cloned.1.call-done), kind=kOutput, calls=%fused_computation.65 | convolution fusion | flops 838860800 | bytes 4751360 | tf_op jit(solution)/shard_map/dot_general | solution.py:97
  118.6 4.1 %fusion.45 = f32[1024,640]{1,0:T(8,128)} fusion(bf16[1024,640]{1,0:T(8,128)(2,1)S(1)} %bitcast.163, bf16[640,1920]{1,0:T(8,128)(2,1)} %all-gather.8.cloned.1.call-done), kind=kOutput, calls=%fused_computation.69 | convolution fusion | flops 838860800 | bytes 4751360 | tf_op jit(solution)/shard_map/dot_general | solution.py:97
  122.7 4.1 fusion.49
  126.9 2.8 fusion.53
  129.7 2.8 fusion.57
  132.4 2.6 fusion.61
  135.1 1.3 fusion.69
  136.5 1.3 fusion.65
  138.3 1.0 copy-done.14
  140.8 4.9 %fusion.3 = bf16[1024,640]{1,0:T(8,128)(2,1)} fusion(bf16[1024,640]{1,0:T(8,128)(2,1)S(1)} %bitcast.169, f32[1024,640]{1,0:T(8,128)S(1)} %copy-done.14, f32[1024,640]{1,0:T(8,128)S(1)} %copy-done.15, f32[1024,640]{1,0:T(8,128)S(1)} %copy-done.16, f32[1024,640]{1,0:T(8,128)S(1)} %copy-done.17, f32[1024,640]{1,0:T(8,128)S(1)} %copy-done.18, ...), kind=kOutput, calls=%fused_computation.19 | convolution fusion | flops 851312640 | bytes 25722880 | tf_op jit(solution)/shard_map/dot_general | solution.py:97
  145.7 10.1 %all-to-all-done.1 = f32[3,8,5,5760]{3,0,2,1:T(4,128)} async-done(((f32[3,8,5,5760]{3,0,2,1:T(4,128)}), f32[3,8,5,5760]{3,0,2,1:T(4,128)}, u32[]{:S(2)}, u32[]{:S(2)}) %all-to-all-start.1) | async-done | bytes 2764832 | tf_op jit(solution)/shard_map/all_to_all | solution.py:56
  155.8 2.4 copy.50
  158.6 1.2 fusion.17
  159.9 1.2 fusion.19
  161.3 1.2 fusion.21
  162.5 1.9 fusion.2
  164.4 2.5 copy.40
  166.9 2.4 copy.39
  169.3 2.5 copy.38
  171.9 3.1 fusion.23
  175.0 1.2 fusion.25
  176.3 1.2 fusion.27
  177.5 1.9 fusion.1
  179.4 2.5 copy.37
  182.0 2.5 copy.36
  184.5 2.5 copy.35
  186.9 3.1 fusion.29
  190.0 1.2 fusion.31
  191.3 1.2 fusion.33
  192.5 1.9 fusion
  194.5 4.5 %fusion.51 = f32[1024,640]{1,0:T(8,128)} fusion(bf16[1024,640]{1,0:T(8,128)(2,1)} %fusion.3, bf16[640,1920]{1,0:T(8,128)(2,1)} %all-gather.6.cloned.1.call-done), kind=kOutput, calls=%fused_computation.75 | convolution fusion | flops 838860800 | bytes 4751360 | tf_op jit(solution)/shard_map/dot_general | solution.py:128
  198.9 4.4 %pad_slice_fusion = (bf16[4,16,16,640]{3,2,1,0:T(8,128)(2,1)}, bf16[4,16,16,640]{3,2,1,0:T(8,128)(2,1)}, bf16[4,16,16,640]{3,2,1,0:T(8,128)(2,1)S(1)}, bf16[4,16...) fusion(bf16[4,16,16,640]{3,2,1,0:T(8,128)(2,1)S(1)} %bitcast.166), kind=kLoop, calls=%fused_computation.9 | loop fusion | bytes 11796480 | tf_op jit(solution)/shard_map/slice | solution.py:32
  203.4 2.8 fusion.39
  206.2 2.9 fusion.43
  209.1 2.9 fusion.47
  212.0 2.9 fusion.55
  214.9 4.0 fusion.59
  218.9 10.3 %reduce-scatter.17.cloned.1.call-done = bf16[1,40,1920]{2,1,0:T(8,128)(2,1)} async-done(((bf16[16,40,1920]{2,1,0:T(8,128)(2,1)}), bf16[1,40,1920]{2,1,0:T(8,128)(2,1)}) %reduce-scatter.17.cloned.1.call-update) | async-done | bytes 153616
  229.2 1.0 concatenate.27
  230.2 65.6 %reduce-scatter.15.cloned.1.call-done = bf16[1,40,1920]{2,1,0:T(8,128)(2,1)} async-done(((bf16[16,40,1920]{2,1,0:T(8,128)(2,1)}), bf16[1,40,1920]{2,1,0:T(8,128)(2,1)}) %reduce-scatter.15.cloned.1.call-update) | async-done | bytes 153616
  296.8 65.7 %reduce-scatter.13.cloned.1.call-done = bf16[1,40,1920]{2,1,0:T(8,128)(2,1)} async-done(((bf16[16,40,1920]{2,1,0:T(8,128)(2,1)}), bf16[1,40,1920]{2,1,0:T(8,128)(2,1)}) %reduce-scatter.13.cloned.1.call-update) | async-done | bytes 153616
  363.4 1.0 maximum_bitcast_fusion
  364.4 6.5 %all-to-all-start.2 = ((bf16[1,8,5,5760]{3,2,0,1:T(8,128)(2,1)}), bf16[1,8,5,5760]{3,2,0,1:T(8,128)(2,1)S(1)}, u32[]{:S(2)}, u32[]{:S(2)}) async-start(bf16[1,8,5,5760]{3,2,0,1:T(8,128)(2,1)} %maximum_bitcast_fusion), calls=%async_computation.2 | async-start | bytes 1474560 | tf_op jit(solution)/shard_map/all_to_all | solution.py:51
  371.0 4.5 %fusion.67 = f32[1024,640]{1,0:T(8,128)} fusion(bf16[1024,640]{1,0:T(8,128)(2,1)} %bitcast.181, bf16[640,1920]{1,0:T(8,128)(2,1)} %all-gather.4.cloned.1.call-done), kind=kOutput, calls=%fused_computation.91 | convolution fusion | flops 838860800 | bytes 4751360 | tf_op jit(solution)/shard_map/dot_general | solution.py:128
  375.4 4.0 fusion.63
  379.4 2.2 all-to-all-done.2
  381.6 1.5 gather_fusion.1
  383.1 2.1 fusion.36
  385.2 5.0 %all-to-all-start.3 = ((bf16[1,8,5,5760]{3,2,0,1:T(8,128)(2,1)}), bf16[1,8,5,5760]{3,2,0,1:T(8,128)(2,1)S(1)}, u32[]{:S(2)}, u32[]{:S(2)}) async-start(bf16[1,8,5,5760]{3,2,0,1:T(8,128)(2,1)} %fusion.36), calls=%async_computation.3 | async-start | bytes 1474560 | tf_op jit(solution)/shard_map/all_to_all | solution.py:56
  390.3 11.3 %fusion.16 = bf16[1024,640]{1,0:T(8,128)(2,1)} fusion(bf16[1,4,16,16,640]{4,3,2,1,0:T(8,128)(2,1)} %param.6, f32[1024,640]{1,0:T(8,128)} %fusion.39, f32[1024,640]{1,0:T(8,128)} %fusion.43, f32[1024,640]{1,0:T(8,128)} %fusion.47, f32[1024,640]{1,0:T(8,128)} %fusion.51, f32[1024,640]{1,0:T(8,128)} %fusion.55, f32[1024,640]{1,0:T(8,128)} %fusion.59, ...), kind=kOutput, calls=%fused_computation.35 | convolution fusion | flops 851312640 | bytes 25722880 | tf_op jit(solution)/shard_map/dot_general | solution.py:128
  401.6 1.1 reshape.204
  402.7 3.0 divide_subtract_fusion
  (91 shorter events, 9.2 us)
Async XLA Ops:
  7.2 3.0 copy-start.13
  7.2 3.0 copy-start.29
  7.2 106.8 %all-gather.8.cloned.1.call-start = ((), (), s32[]{:S(2)}) async-start(), calls=%async_computation.9 | async-start | bytes 2611200 | tf_op jit(solution)/shard_map/all_gather | solution.py:65
  9.4 113.3 %all-gather.6.cloned.1.call-start = ((), (), s32[]{:S(2)}) async-start(), calls=%async_computation.8 | async-start | bytes 2611200 | tf_op jit(solution)/shard_map/all_gather | solution.py:65
  14.3 8.8 %copy-start = (bf16[1,4,16,16,640]{4,3,2,1,0:T(8,128)(2,1)S(1)}, bf16[1,4,16,16,640]{4,3,2,1,0:T(8,128)(2,1)}, u32[]{:S(2)}) copy-start(bf16[1,4,16,16,640]{4,3,2,1,0:T(8,128)(2,1)} %param.6) | copy-start | bytes 3932164
  14.3 73.5 %all-to-all-start = ((f32[3,8,5,5760]{3,0,2,1:T(4,128)}), f32[3,8,5,5760]{3,0,2,1:T(4,128)}, u32[]{:S(2)}, u32[]{:S(2)}) async-start(f32[3,8,5,5760]{3,0,2,1:T(4,128)} %bitcast.147), calls=%async_computation | async-start | bytes 7372800 | tf_op jit(solution)/shard_map/all_to_all | solution.py:51
  22.3 110.1 %all-gather.4.cloned.1.call-start = ((), (), s32[]{:S(2)}) async-start(), calls=%async_computation.7 | async-start | bytes 2611200 | tf_op jit(solution)/shard_map/all_gather | solution.py:65
  23.8 0.9 copy-start.33
  98.9 57.0 %all-to-all-start.1 = ((f32[3,8,5,5760]{3,0,2,1:T(4,128)}), f32[3,8,5,5760]{3,0,2,1:T(4,128)}, u32[]{:S(2)}, u32[]{:S(2)}) async-start(f32[3,8,5,5760]{3,0,2,1:T(4,128)} %select_bitcast_fusion), calls=%async_computation.1 | async-start | bytes 7372800 | tf_op jit(solution)/shard_map/all_to_all | solution.py:56
  103.4 125.8 %reduce-scatter.17.cloned.1.call-start = ((), (), s32[]{:S(2)}) async-start(), calls=%async_computation.12 | async-start | bytes 2611200
  108.4 4.0 copy-start.7
  114.0 4.6 %copy-start.8 = (bf16[4,16,16,640]{3,2,1,0:T(8,128)(2,1)S(1)}, bf16[4,16,16,640]{3,2,1,0:T(8,128)(2,1)}, u32[]{:S(2)}) copy-start(bf16[4,16,16,640]{3,2,1,0:T(8,128)(2,1)} %get-tuple-element.17) | copy-start | bytes 3932164
  118.6 4.1 %copy-start.6 = (bf16[4,16,16,640]{3,2,1,0:T(8,128)(2,1)S(1)}, bf16[4,16,16,640]{3,2,1,0:T(8,128)(2,1)}, u32[]{:S(2)}) copy-start(bf16[4,16,16,640]{3,2,1,0:T(8,128)(2,1)} %get-tuple-element.18) | copy-start | bytes 3932164
  122.7 4.1 copy-start.5
  122.7 4.1 copy-start.31
  126.9 2.8 copy-start.4
  129.7 2.8 copy-start.3
  132.4 2.6 copy-start.1
  132.4 2.6 copy-start.30
  135.1 1.4 copy-start.2
  135.1 2.7 copy-start.17
  135.1 2.9 copy-start.18
  135.1 3.2 copy-start.19
  136.4 2.9 copy-start.14
  136.4 3.7 copy-start.15
  136.5 4.4 %copy-start.16 = (f32[1024,640]{1,0:T(8,128)S(1)}, f32[1024,640]{1,0:T(8,128)}, u32[]{:S(2)}) copy-start(f32[1024,640]{1,0:T(8,128)} %fusion.49) | copy-start | bytes 7864324
  155.8 2.4 copy-start.9
  155.8 2.8 copy-start.22
  158.6 1.3 copy-start.21
  159.9 1.3 copy-start.20
  164.4 131.5 %reduce-scatter.15.cloned.1.call-start = ((), (), s32[]{:S(2)}) async-start(), calls=%async_computation.11 | async-start | bytes 2611200
  171.9 3.1 copy-start.10
  171.9 3.1 copy-start.23
  175.0 1.3 copy-start.24
  179.4 183.1 %reduce-scatter.13.cloned.1.call-start = ((), (), s32[]{:S(2)}) async-start(), calls=%async_computation.10 | async-start | bytes 2611200
  186.9 3.1 copy-start.11
  186.9 3.1 copy-start.25
  190.0 1.3 copy-start.26
  194.5 4.5 %copy-start.12 = (bf16[1024,640]{1,0:T(8,128)(2,1)S(1)}, bf16[1024,640]{1,0:T(8,128)(2,1)}, u32[]{:S(2)}) copy-start(bf16[1024,640]{1,0:T(8,128)(2,1)} %fusion.3) | copy-start | bytes 3932164
  198.9 4.4 %copy-start.28 = (bf16[640,1920]{1,0:T(8,128)(2,1)S(1)}, bf16[640,1920]{1,0:T(8,128)(2,1)}, u32[]{:S(2)}) copy-start(bf16[640,1920]{1,0:T(8,128)(2,1)} %all-gather.8.cloned.1.call-done) | copy-start | bytes 7372804
  206.2 2.9 copy-start.32
  364.4 17.2 %all-to-all-start.2 = ((bf16[1,8,5,5760]{3,2,0,1:T(8,128)(2,1)}), bf16[1,8,5,5760]{3,2,0,1:T(8,128)(2,1)S(1)}, u32[]{:S(2)}, u32[]{:S(2)}) async-start(bf16[1,8,5,5760]{3,2,0,1:T(8,128)(2,1)} %maximum_bitcast_fusion), calls=%async_computation.2 | async-start | bytes 1474560 | tf_op jit(solution)/shard_map/all_to_all | solution.py:51
  371.0 4.5 %copy-start.27 = (bf16[4,16,16,640]{3,2,1,0:T(8,128)(2,1)S(1)}, bf16[4,16,16,640]{3,2,1,0:T(8,128)(2,1)}, u32[]{:S(2)}) copy-start(bf16[4,16,16,640]{3,2,1,0:T(8,128)(2,1)} %get-tuple-element.25) | copy-start | bytes 3932164
  385.2 16.4 %all-to-all-start.3 = ((bf16[1,8,5,5760]{3,2,0,1:T(8,128)(2,1)}), bf16[1,8,5,5760]{3,2,0,1:T(8,128)(2,1)S(1)}, u32[]{:S(2)}, u32[]{:S(2)}) async-start(bf16[1,8,5,5760]{3,2,0,1:T(8,128)(2,1)} %fusion.36), calls=%async_computation.3 | async-start | bytes 1474560 | tf_op jit(solution)/shard_map/all_to_all | solution.py:56
Sparse Core Ops, SparseCore 0:
  10.3 39.3 all-gather.7
  52.0 36.3 all-gather.5
  90.7 37.1 all-gather.3
  164.5 64.6 reduce-scatter.16
  231.5 64.3 reduce-scatter.14
  298.1 64.3 reduce-scatter.12
